TPU v7x, 512 devices: a whole 4x4x16 slice. The times are simulated.
512 devices in a mesh: blk: 64 (over y_lo, z, core), exp: 8 (over y_hi, x).
Axes of the slice: x: 4, y: 4 (y_hi: 2, y_lo: 2; y = y_hi * 2 + y_lo), z: 16, core: 2. Of those that a mesh axis runs over, the one named last changes fastest.
Arguments:
- hidden_in: bfloat16 [32, 4, 2048], P('exp'), may hold values from -3 to 3
- q_lat: bfloat16 [32, 4, 16, 512], P('exp'), may hold values from -28 to 28
- q_rope: bfloat16 [32, 4, 16, 64], P('exp'), may hold values from -4 to 4
- new_lat: bfloat16 [32, 4, 512], P('exp'), may hold values from -4 to 4
- new_rope: bfloat16 [32, 4, 64], P('exp'), may hold values from -4 to 4
- cache_lat: bfloat16 [32, 16384, 512], P('exp', 'blk'), may hold values from -4 to 4
- cache_rope: bfloat16 [32, 16384, 64], P('exp', 'blk'), may hold values from -4 to 4
- lengths: int32 [32], P('exp'), may hold values from 2 to 16384, as said below
- w_uv: bfloat16 [512, 2048], P(None, 'blk'), may hold values from -3 to 3
- w_out: bfloat16 [2048, 2048], P('blk'), may hold values from -0.125 to 0.125
- norm_gain: float32 [2048], replicated, may hold values from 0.1 to 1.9
- w_router: bfloat16 [2048, 64], replicated, may hold values from -0.125 to 0.125
- routes: int32 [32, 4, 6], P('exp'), may hold values from 0 to 63, all different within a row; in each aligned block of 16 rows (0 to 15, 16 to 31, ..., all dimensions but the last counted through in order) at most 3 rows name the same one
- w_gate: bfloat16 [64, 2048, 1408], P('blk', None, 'exp'), may hold values from -0.125 to 0.125
- w_up: bfloat16 [64, 2048, 1408], P('blk', None, 'exp'), may hold values from -0.125 to 0.125
- w_down: bfloat16 [64, 1408, 2048], P('blk', 'exp'), may hold values from -0.15625 to 0.15625
Outputs:
- hidden_out: bfloat16 [32, 4, 2048], P('exp')
Inputs may be any that keep to these rules, and one draw needn't show every extreme that they name: `lengths`: in each aligned group of 4 requests exactly 1 have length 16384; the others have 2 to 512. `routes`: each row names 6 different experts; in the 16 rows of one index of exp no expert is named more than 3 times.
All inputs are finite; a program needn't handle non-finite values.
Results may differ from a plain program's by a relative error of at most 0.0062.
Values may be sent and summed in bfloat16 or wider, within the bound.
No kernel may reach another device: no remote copies, remote signals or barrier semaphores. Data moves between devices by JAX's collectives and lax.ppermute only.
A program may use at most 128 MiB of HBM per device.

v0:
```python
import jax
import jax.numpy as jnp
from jax import lax
from jax.sharding import PartitionSpec as P

V = 128
QK = 192
CAP = 3
NEG_FILL = -1e30
ROUTE_SCALE = 2.446
NORM_EPS = 1e-06


def xor_pairs(count, mask):
    return [(i, i ^ mask) for i in range(count)]


def exchange(x, axis, mask):
    count = lax.axis_size(axis)
    return jax.tree.map(lambda part: lax.ppermute(part, axis, xor_pairs(count, mask)), x)


def exchange_state(state, axis, mask):
    peak_val, weight_sum, summed = state
    packed = jnp.concatenate([summed, peak_val[..., None], weight_sum[..., None]], axis=-1)
    got = exchange(packed, axis, mask)
    width = summed.shape[-1]
    return (got[..., width], got[..., width + 1], got[..., :width])


def butterfly_sum(x, axis, bits):
    for bit in bits:
        x = x + exchange(x, axis, 1 << bit)
    return x


def butterfly_gather(x, axis, bits):
    me = lax.axis_index(axis)
    x = x[None]
    for bit in bits:
        other = exchange(x, axis, 1 << bit)
        high = me >> bit & 1 == 1
        low_part = jnp.where(high, other, x)
        high_part = jnp.where(high, x, other)
        x = jnp.concatenate([low_part, high_part], axis=0)
    return x


def butterfly_scatter_sum(x, axis, bits):
    me = lax.axis_index(axis)
    for bit in bits:
        side = me >> bit & 1
        keep = lax.dynamic_index_in_dim(x, side, 0, keepdims=False)
        send = lax.dynamic_index_in_dim(x, 1 - side, 0, keepdims=False)
        x = keep + exchange(send, axis, 1 << bit)
    return x


def block_partial(query, query_rope, keys_lat, keys_rope, valid):
    scale = QK ** (-0.5)
    scores = (
        jnp.einsum("rmc,rkc->rmk", query, keys_lat, preferred_element_type=jnp.float32)
        + jnp.einsum("rmc,rkc->rmk", query_rope, keys_rope, preferred_element_type=jnp.float32)
    ) * scale
    masked = jnp.where(valid, scores, NEG_FILL)
    peak_val = jnp.max(masked, axis=2)
    weights = jnp.where(valid, jnp.exp(masked - peak_val[:, :, None]), 0.0)
    weight_sum = jnp.sum(weights, axis=2)
    summed = jnp.einsum(
        "rmk,rkc->rmc", weights.astype(jnp.bfloat16), keys_lat, preferred_element_type=jnp.float32
    )
    return (peak_val, weight_sum, summed)


def merge_pair(left_part, right_part):
    peak_left, total_left, sum_left = left_part
    peak_right, total_right, sum_right = right_part
    peak_val = jnp.maximum(peak_left, peak_right)
    factor_left = jnp.exp(peak_left - peak_val)
    factor_right = jnp.exp(peak_right - peak_val)
    weight_sum = factor_left * total_left + factor_right * total_right
    summed = factor_left[..., None] * sum_left + factor_right[..., None] * sum_right
    return (peak_val, weight_sum, summed)


def local(
    hidden_in,
    q_lat,
    q_rope,
    new_lat,
    new_rope,
    cache_lat,
    cache_rope,
    lengths,
    w_uv,
    w_out,
    norm_gain,
    w_router,
    routes,
    w_gate,
    w_up,
    w_down,
):
    requests, new_steps, head_count, latent_dim = q_lat.shape
    me = lax.axis_index("blk")
    blk_bits = lax.axis_size("blk").bit_length() - 1
    exp_bits = lax.axis_size("exp").bit_length() - 1
    query_rows = new_steps * head_count
    query = q_lat.reshape(requests, query_rows, latent_dim)
    query_rope = q_rope.reshape(requests, query_rows, q_rope.shape[3])
    cache_span = cache_lat.shape[1]
    position = me * cache_span + lax.iota(jnp.int32, cache_span)
    cache_valid = jnp.broadcast_to(
        position[None, None, :] < lengths[:, None, None], (requests, query_rows, cache_span)
    )
    peak_val, weight_sum, summed = block_partial(
        query, query_rope, cache_lat, cache_rope, cache_valid
    )
    head_bits = head_count.bit_length() - 1
    split = (2,) * head_bits
    state = (
        peak_val.reshape(requests, new_steps, head_count)
        .transpose(2, 0, 1)
        .reshape(split + (requests, new_steps)),
        weight_sum.reshape(requests, new_steps, head_count)
        .transpose(2, 0, 1)
        .reshape(split + (requests, new_steps)),
        summed.reshape(requests, new_steps, head_count, latent_dim)
        .transpose(2, 0, 1, 3)
        .reshape(split + (requests, new_steps, latent_dim)),
    )
    low_bits = blk_bits - head_bits
    order = [head_bits - 1] + list(range(head_bits - 1))
    remaining = list(range(head_bits - 1, -1, -1))
    for head_bit in order:
        axis_pos = remaining.index(head_bit)
        remaining.pop(axis_pos)
        bit = head_bit + low_bits
        side = me >> bit & 1
        keep = jax.tree.map(
            lambda part: lax.dynamic_index_in_dim(part, side, axis_pos, keepdims=False), state
        )
        send = jax.tree.map(
            lambda part: lax.dynamic_index_in_dim(part, 1 - side, axis_pos, keepdims=False), state
        )
        state = merge_pair(keep, exchange_state(send, "blk", 1 << bit))
    for bit in range(low_bits - 1, -1, -1):
        state = merge_pair(state, exchange_state(state, "blk", 1 << bit))
    head_pick = me >> low_bits
    own_query = lax.dynamic_index_in_dim(q_lat, head_pick, axis=2, keepdims=False)
    own_rope = lax.dynamic_index_in_dim(q_rope, head_pick, axis=2, keepdims=False)
    fresh_valid = lax.iota(jnp.int32, new_steps)[None, :] <= lax.iota(jnp.int32, new_steps)[:, None]
    fresh_valid = jnp.broadcast_to(fresh_valid[None, :, :], (requests, new_steps, new_steps))
    fresh_part = block_partial(own_query, own_rope, new_lat, new_rope, fresh_valid)
    peak_val, weight_sum, summed = merge_pair(state, fresh_part)
    lat_out = (summed / weight_sum[:, :, None]).astype(jnp.bfloat16)
    token_rows = requests * new_steps
    lat_head = lat_out.reshape(token_rows, latent_dim)
    heads_out = jnp.dot(lat_head, w_uv, preferred_element_type=jnp.float32).astype(jnp.bfloat16)
    proj_part = jnp.dot(heads_out, w_out, preferred_element_type=jnp.float32)
    projected = butterfly_sum(proj_part, "blk", range(blk_bits))
    width = hidden_in.shape[2]
    mixed = hidden_in.reshape(token_rows, width).astype(jnp.float32) + projected
    meansq = jnp.mean(mixed * mixed, axis=1, keepdims=True)
    normed = (mixed * lax.rsqrt(meansq + NORM_EPS) * norm_gain[None, :]).astype(jnp.bfloat16)
    affinity = jax.nn.sigmoid(jnp.dot(normed, w_router, preferred_element_type=jnp.float32))
    expert_total = w_router.shape[1]
    top_count = routes.shape[2]
    flat_routes = routes.reshape(token_rows, top_count)
    route_hits = flat_routes[:, :, None] == lax.iota(jnp.int32, expert_total)[None, None, :]
    chosen = jnp.sum(jnp.where(route_hits, affinity[:, None, :], 0.0), axis=2)
    route_weight = ROUTE_SCALE * chosen / jnp.sum(chosen, axis=1, keepdims=True)
    local_count = w_gate.shape[0]
    local_ids = me * local_count + lax.iota(jnp.int32, local_count)
    pair_routes = flat_routes.reshape(token_rows * top_count)
    local_hits = (pair_routes[:, None] == local_ids[None, :]).astype(jnp.int32)
    ranks = jnp.cumsum(local_hits, axis=0) - 1
    slot_ids = lax.iota(jnp.int32, CAP)
    slot_match = local_hits.T[:, None, :] * (ranks.T[:, None, :] == slot_ids[None, :, None]).astype(
        jnp.int32
    )
    select = slot_match.reshape(local_count, CAP, token_rows, top_count).astype(jnp.float32)
    dispatch_map = jnp.sum(select, axis=3)
    combine_map = jnp.sum(select * route_weight[None, None, :, :], axis=3)
    dispatched = jnp.einsum(
        "esr,rd->esd", dispatch_map.astype(jnp.bfloat16), normed, preferred_element_type=jnp.float32
    ).astype(jnp.bfloat16)
    gate_w = lax.all_gather(w_gate, "exp", axis=2, tiled=True)
    up_w = lax.all_gather(w_up, "exp", axis=2, tiled=True)
    down_w = lax.all_gather(w_down, "exp", axis=1, tiled=True)
    gate = jnp.einsum("erd,edf->erf", dispatched, gate_w, preferred_element_type=jnp.float32)
    upper = jnp.einsum("erd,edf->erf", dispatched, up_w, preferred_element_type=jnp.float32)
    hidden_all = (jax.nn.silu(gate) * upper).astype(jnp.bfloat16)
    expert_out = jnp.einsum("erf,efd->erd", hidden_all, down_w, preferred_element_type=jnp.float32)
    moe_part = jnp.einsum("esr,esd->rd", combine_map, expert_out, precision=lax.Precision.HIGHEST)
    moe_all = butterfly_sum(moe_part, "blk", range(blk_bits))
    result = (mixed + moe_all).astype(jnp.bfloat16)
    return result.reshape(requests, new_steps, width)


def solution(mesh):
    in_specs = (
        P("exp", None, None),
        P("exp", None, None, None),
        P("exp", None, None, None),
        P("exp", None, None),
        P("exp", None, None),
        P("exp", "blk", None),
        P("exp", "blk", None),
        P("exp"),
        P(None, "blk"),
        P("blk", None),
        P(),
        P(),
        P("exp", None, None),
        P("blk", None, "exp"),
        P("blk", None, "exp"),
        P("blk", "exp", None),
    )
    out_specs = P("exp", None, None)
    return jax.shard_map(local, mesh=mesh, in_specs=in_specs, out_specs=out_specs, check_vma=False)
```

profile of v0, /device:TPU:8, one launch (start us, length us, event | category | flops | bytes accessed | tf_op | source)
XLA Modules:
  0.0 402.4 jit_solution(3735238704035035130)
XLA Ops:
  6.5 0.7 all-gather.4.cloned.1.call-update
  7.3 0.7 all-gather.6.cloned.1.call-update
  8.1 0.7 all-gather.8.cloned.1.call-update
  8.8 0.7 broadcast_compare_fusion
  9.5 1.4 fusion.115
  10.9 1.2 fusion.113
  12.1 0.2 fusion.23
  12.4 0.3 fusion.25
  13.0 0.3 copy.117
  13.3 0.3 copy.142
  13.8 0.3 copy.116
  14.3 7.7 %collective-permute-start = (f32[2,2,2,4,4,514]{5,4,3,2,1,0:T(4,128)S(1)}, f32[2,2,2,4,4,514]{5,4,3,2,1,0:T(4,128)S(1)}, u32[]{:S(2)}, u32[]{:S(2)}) collective-permute-start(f32[2,2,2,4,4,514]{5,4,3,2,1,0:T(4,128)S(1)} %pad_maximum_fusion), channel_id=1, source_target_pairs={{0,256},{8,264},{16,272},{24,280},{32,288},{40,296},{48,304},{56,3... | collective-permute-start | bytes 789512 | tf_op jit(solution)/shard_map/ppermute | solution.py:20
  22.0 0.9 constant_dynamic-slice_fusion.1
  22.9 4.1 %collective-permute-done = f32[2,2,2,4,4,514]{5,4,3,2,1,0:T(4,128)S(1)} collective-permute-done((f32[2,2,2,4,4,514]{5,4,3,2,1,0:T(4,128)S(1)}, f32[2,2,2,4,4,514]{5,4,3,2,1,0:T(4,128)S(1)}, u32[]{:S(2)}, u32[]{:S(2)}) %collective-permute-start) | collective-permute-done | bytes 263200 | tf_op jit(solution)/shard_map/ppermute | solution.py:20
  27.0 0.2 fusion.110
  27.2 0.3 copy.145
  27.6 0.2 copy.121
  27.8 0.2 copy.122
  28.3 3.8 collective-permute-start.1
  32.2 6.7 %collective-permute-done.1 = f32[2,2,4,4,514]{4,3,2,1,0:T(4,128)S(1)} collective-permute-done((f32[2,2,4,4,514]{4,3,2,1,0:T(4,128)S(1)}, f32[2,2,4,4,514]{4,3,2,1,0:T(4,128)S(1)}, u32[]{:S(2)}, u32[]{:S(2)}) %collective-permute-start.1) | collective-permute-done | bytes 131616 | tf_op jit(solution)/shard_map/ppermute | solution.py:20
  39.8 9.1 %collective-permute-start.2 = (f32[2,4,4,514]{3,2,1,0:T(4,128)S(1)}, f32[2,4,4,514]{3,2,1,0:T(4,128)S(1)}, u32[]{:S(2)}, u32[]{:S(2)}) collective-permute-start(f32[2,4,4,514]{3,2,1,0:T(4,128)S(1)} %pad_maximum_fusion.2), channel_id=1, source_target_pairs={{0,64},{8,72},{16,80},{24,88},{32,96},{40,104},{48,112},{56,120},{... | collective-permute-start | bytes 197384 | tf_op jit(solution)/shard_map/ppermute | solution.py:20
  48.9 0.8 constant_dynamic-slice_fusion
  49.7 5.0 %collective-permute-done.2 = f32[2,4,4,514]{3,2,1,0:T(4,128)S(1)} collective-permute-done((f32[2,4,4,514]{3,2,1,0:T(4,128)S(1)}, f32[2,4,4,514]{3,2,1,0:T(4,128)S(1)}, u32[]{:S(2)}, u32[]{:S(2)}) %collective-permute-start.2) | collective-permute-done | bytes 65824 | tf_op jit(solution)/shard_map/ppermute | solution.py:20
  55.5 13.7 %collective-permute-start.3 = (f32[4,4,514]{2,1,0:T(4,128)S(1)}, f32[4,4,514]{2,1,0:T(4,128)S(1)}, u32[]{:S(2)}, u32[]{:S(2)}) collective-permute-start(f32[4,4,514]{2,1,0:T(4,128)S(1)} %pad_maximum_fusion.3), channel_id=1, source_target_pairs={{0,128},{8,136},{16,144},{24,152},{32,160},{40,168},{48,176},{56,1... | collective-permute-start | bytes 98696 | tf_op jit(solution)/shard_map/ppermute | solution.py:20
  69.4 1.7 collective-permute-done.3
  71.5 1.9 collective-permute-start.4
  73.6 3.8 collective-permute-done.4
  77.7 1.9 collective-permute-start.5
  79.9 0.9 collective-permute-done.5
  81.0 0.2 fusion.38
  81.3 0.3 fusion.19
  81.5 2.1 collective-permute-start.6
  83.6 1.2 collective-permute-done.6
  84.8 1.9 collective-permute-start.7
  86.7 5.5 %collective-permute-done.7 = f32[16,2048]{1,0:T(8,128)S(1)} collective-permute-done((f32[16,2048]{1,0:T(8,128)S(1)}, f32[16,2048]{1,0:T(8,128)S(1)}, u32[]{:S(2)}, u32[]{:S(2)}) %collective-permute-start.7) | collective-permute-done | bytes 131104 | tf_op jit(solution)/shard_map/ppermute | solution.py:20
  92.3 1.9 collective-permute-start.8
  94.2 8.5 %collective-permute-done.8 = f32[16,2048]{1,0:T(8,128)S(1)} collective-permute-done((f32[16,2048]{1,0:T(8,128)S(1)}, f32[16,2048]{1,0:T(8,128)S(1)}, u32[]{:S(2)}, u32[]{:S(2)}) %collective-permute-start.8) | collective-permute-done | bytes 131104 | tf_op jit(solution)/shard_map/ppermute | solution.py:20
  102.7 6.4 %collective-permute-start.9 = (f32[16,2048]{1,0:T(8,128)S(1)}, f32[16,2048]{1,0:T(8,128)S(1)}, u32[]{:S(2)}, u32[]{:S(2)}) collective-permute-start(f32[16,2048]{1,0:T(8,128)S(1)} %add.218), channel_id=1, source_target_pairs={{0,64},{8,72},{16,80},{24,88},{32,96},{40,104},{48,112},{56,120},{... | collective-permute-start | bytes 393224 | tf_op jit(solution)/shard_map/ppermute | solution.py:20
  109.1 12.2 %collective-permute-done.9 = f32[16,2048]{1,0:T(8,128)S(1)} collective-permute-done((f32[16,2048]{1,0:T(8,128)S(1)}, f32[16,2048]{1,0:T(8,128)S(1)}, u32[]{:S(2)}, u32[]{:S(2)}) %collective-permute-start.9) | collective-permute-done | bytes 131104 | tf_op jit(solution)/shard_map/ppermute | solution.py:20
  121.3 10.5 %collective-permute-start.10 = (f32[16,2048]{1,0:T(8,128)S(1)}, f32[16,2048]{1,0:T(8,128)S(1)}, u32[]{:S(2)}, u32[]{:S(2)}) collective-permute-start(f32[16,2048]{1,0:T(8,128)S(1)} %add.219), channel_id=1, source_target_pairs={{0,128},{8,136},{16,144},{24,152},{32,160},{40,168},{48,176},{56,1... | collective-permute-start | bytes 393224 | tf_op jit(solution)/shard_map/ppermute | solution.py:20
  131.9 12.3 %collective-permute-done.10 = f32[16,2048]{1,0:T(8,128)S(1)} collective-permute-done((f32[16,2048]{1,0:T(8,128)S(1)}, f32[16,2048]{1,0:T(8,128)S(1)}, u32[]{:S(2)}, u32[]{:S(2)}) %collective-permute-start.10) | collective-permute-done | bytes 131104 | tf_op jit(solution)/shard_map/ppermute | solution.py:20
  144.2 2.4 collective-permute-start.11
  146.9 0.3 reduce_window_sum.11
  147.4 3.7 collective-permute-done.11
  151.3 0.2 fusion.16
  151.5 0.2 select_reduce_fusion
  152.0 4.2 %fusion.4 = f32[3,1408]{1,0:T(4,128)S(1)} fusion(bf16[3,2048]{1,0:T(4,128)(2,1)S(1)} %convolution_convert_fusion, bf16[1,2048,1408]{1,2,0:T(8,128)(2,1)} %all-gather.4.cloned.1.call-done), kind=kOutput, calls=%fused_computation.4 | convolution fusion | flops 17301504 | bytes 5796352 | tf_op jit(solution)/shard_map/erd,edf->erf/dot_general | solution.py:191
  156.2 61.2 %all-gather.6.cloned.1.call-done = bf16[1,2048,1408]{1,2,0:T(8,128)(2,1)} async-done(((bf16[1,2048,176]{1,2,0:T(8,128)(2,1)}), bf16[1,2048,1408]{1,2,0:T(8,128)(2,1)}) %all-gather.6.cloned.1.call-update) | async-done | bytes 5767184 | tf_op jit(solution)/shard_map/all_gather | solution.py:189
  217.4 100.9 %all-gather.8.cloned.1.call-done = bf16[1,1408,2048]{2,1,0:T(8,128)(2,1)} async-done(((bf16[1,176,2048]{2,1,0:T(8,128)(2,1)}), bf16[1,1408,2048]{2,1,0:T(8,128)(2,1)}) %all-gather.8.cloned.1.call-update) | async-done | bytes 5767184 | tf_op jit(solution)/shard_map/all_gather | solution.py:190
  318.4 7.0 %fusion = f32[3,2048]{1,0:T(4,128)S(1)} fusion(bf16[1,1408,2048]{2,1,0:T(8,128)(2,1)} %all-gather.8.cloned.1.call-done, bf16[3,2048]{1,0:T(4,128)(2,1)S(1)} %convolution_convert_fusion, bf16[1,2048,1408]{1,2,0:T(8,128)(2,1)} %all-gather.6.cloned.1.call-done, f32[3,1408]{1,0:T(4,128)S(1)} %fusion.4), kind=kOutput, calls=%fused_computation | convolution fusion | flops 34628352 | bytes 11588096 | tf_op jit(solution)/shard_map/erf,efd->erd/dot_general | solution.py:194
  325.4 0.4 fusion.116
  325.7 1.9 collective-permute-start.12
  327.7 1.3 collective-permute-done.12
  329.0 3.5 collective-permute-start.13
  332.5 4.0 collective-permute-done.13
  336.5 4.5 %collective-permute-start.14 = (f32[16,2048]{1,0:T(8,128)S(1)}, f32[16,2048]{1,0:T(8,128)S(1)}, u32[]{:S(2)}, u32[]{:S(2)}) collective-permute-start(f32[16,2048]{1,0:T(8,128)S(1)} %add.227), channel_id=1, source_target_pairs={{0,32},{8,40},{16,48},{24,56},{32,0},{40,8},{48,16},{56,24},{64,96... | collective-permute-start | bytes 393224 | tf_op jit(solution)/shard_map/ppermute | solution.py:20
  340.9 5.8 %collective-permute-done.14 = f32[16,2048]{1,0:T(8,128)S(1)} collective-permute-done((f32[16,2048]{1,0:T(8,128)S(1)}, f32[16,2048]{1,0:T(8,128)S(1)}, u32[]{:S(2)}, u32[]{:S(2)}) %collective-permute-start.14) | collective-permute-done | bytes 131104 | tf_op jit(solution)/shard_map/ppermute | solution.py:20
  346.8 7.6 %collective-permute-start.15 = (f32[16,2048]{1,0:T(8,128)S(1)}, f32[16,2048]{1,0:T(8,128)S(1)}, u32[]{:S(2)}, u32[]{:S(2)}) collective-permute-start(f32[16,2048]{1,0:T(8,128)S(1)} %add.228), channel_id=1, source_target_pairs={{0,64},{8,72},{16,80},{24,88},{32,96},{40,104},{48,112},{56,120},{... | collective-permute-start | bytes 393224 | tf_op jit(solution)/shard_map/ppermute | solution.py:20
  354.4 9.9 %collective-permute-done.15 = f32[16,2048]{1,0:T(8,128)S(1)} collective-permute-done((f32[16,2048]{1,0:T(8,128)S(1)}, f32[16,2048]{1,0:T(8,128)S(1)}, u32[]{:S(2)}, u32[]{:S(2)}) %collective-permute-start.15) | collective-permute-done | bytes 131104 | tf_op jit(solution)/shard_map/ppermute | solution.py:20
  364.4 12.0 %collective-permute-start.16 = (f32[16,2048]{1,0:T(8,128)S(1)}, f32[16,2048]{1,0:T(8,128)S(1)}, u32[]{:S(2)}, u32[]{:S(2)}) collective-permute-start(f32[16,2048]{1,0:T(8,128)S(1)} %add.229), channel_id=1, source_target_pairs={{0,128},{8,136},{16,144},{24,152},{32,160},{40,168},{48,176},{56,1... | collective-permute-start | bytes 393224 | tf_op jit(solution)/shard_map/ppermute | solution.py:20
  376.4 12.0 %collective-permute-done.16 = f32[16,2048]{1,0:T(8,128)S(1)} collective-permute-done((f32[16,2048]{1,0:T(8,128)S(1)}, f32[16,2048]{1,0:T(8,128)S(1)}, u32[]{:S(2)}, u32[]{:S(2)}) %collective-permute-start.16) | collective-permute-done | bytes 131104 | tf_op jit(solution)/shard_map/ppermute | solution.py:20
  388.4 3.3 collective-permute-start.17
  391.7 3.5 collective-permute-done.17
  395.2 0.7 reshape.304
  (102 shorter events, 5.3 us)
Async XLA Ops:
  6.5 3.0 copy-start
  6.5 25.5 %copy-start.7 = (bf16[4,4,512]{2,1,0:T(4,128)(2,1)S(1)}, bf16[4,4,512]{2,1,0:T(4,128)(2,1)}, u32[]{:S(2)}) copy-start(bf16[4,4,512]{2,1,0:T(4,128)(2,1)} %param.19) | copy-start | bytes 49156
  6.5 145.5 %all-gather.4.cloned.1.call-start = ((), (), s32[]{:S(2)}) async-start(), calls=%async_computation | async-start | bytes 6488064 | tf_op jit(solution)/shard_map/all_gather | solution.py:188
  7.3 210.1 %all-gather.6.cloned.1.call-start = ((), (), s32[]{:S(2)}) async-start(), calls=%async_computation.1 | async-start | bytes 6488064 | tf_op jit(solution)/shard_map/all_gather | solution.py:189
  8.0 310.3 %all-gather.8.cloned.1.call-start = ((), (), s32[]{:S(2)}) async-start(), calls=%async_computation.2 | async-start | bytes 6488064 | tf_op jit(solution)/shard_map/all_gather | solution.py:190
  8.7 64.7 %copy-start.8 = (bf16[4,4,64]{2,1,0:T(4,128)(2,1)S(1)}, bf16[4,4,64]{2,1,0:T(4,128)(2,1)}, u32[]{:S(2)}) copy-start(bf16[4,4,64]{2,1,0:T(4,128)(2,1)} %param.20) | copy-start | bytes 6148
  9.5 71.7 %copy-start.2 = (bf16[32,2048]{1,0:T(8,128)(2,1)S(1)}, bf16[32,2048]{1,0:T(8,128)(2,1)}, u32[]{:S(2)}) copy-start(bf16[32,2048]{1,0:T(8,128)(2,1)} %param.25) | copy-start | bytes 393220
  9.5 71.7 %copy-start.5 = (bf16[512,32]{0,1:T(8,128)(2,1)S(1)}, bf16[512,32]{0,1:T(8,128)(2,1)}, u32[]{:S(2)}) copy-start(bf16[512,32]{0,1:T(8,128)(2,1)} %param.24) | copy-start | bytes 98308
  12.3 119.5 %copy-start.3 = (s32[4,4,6]{2,1,0:T(4,128)S(1)}, s32[4,4,6]{2,1,0:T(4,128)}, u32[]{:S(2)}) copy-start(s32[4,4,6]{2,1,0:T(4,128)} %param.28) | copy-start | bytes 1156
  12.3 134.3 %copy-start.4 = (bf16[4,4,2048]{2,1,0:T(4,128)(2,1)S(1)}, bf16[4,4,2048]{2,1,0:T(4,128)(2,1)}, u32[]{:S(2)}) copy-start(bf16[4,4,2048]{2,1,0:T(4,128)(2,1)} %param.16) | copy-start | bytes 196612
  12.7 138.5 %copy-start.1 = (bf16[2048,64]{0,1:T(8,128)(2,1)S(1)}, bf16[2048,64]{0,1:T(8,128)(2,1)}, u32[]{:S(2)}) copy-start(bf16[2048,64]{0,1:T(8,128)(2,1)} %param.27) | copy-start | bytes 786436
  12.7 138.5 %copy-start.6 = (f32[2048]{0:T(1024)S(1)}, f32[2048]{0:T(1024)}, u32[]{:S(2)}) copy-start(f32[2048]{0:T(1024)} %param.26) | copy-start | bytes 24580
  14.3 12.8 %collective-permute-start = (f32[2,2,2,4,4,514]{5,4,3,2,1,0:T(4,128)S(1)}, f32[2,2,2,4,4,514]{5,4,3,2,1,0:T(4,128)S(1)}, u32[]{:S(2)}, u32[]{:S(2)}) collective-permute-start(f32[2,2,2,4,4,514]{5,4,3,2,1,0:T(4,128)S(1)} %pad_maximum_fusion), channel_id=1, source_target_pairs={{0,256},{8,264},{16,272},{24,280},{32,288},{40,296},{48,304},{56,3... | collective-permute-start | bytes 789512 | tf_op jit(solution)/shard_map/ppermute | solution.py:20
  28.3 10.6 %collective-permute-start.1 = (f32[2,2,4,4,514]{4,3,2,1,0:T(4,128)S(1)}, f32[2,2,4,4,514]{4,3,2,1,0:T(4,128)S(1)}, u32[]{:S(2)}, u32[]{:S(2)}) collective-permute-start(f32[2,2,4,4,514]{4,3,2,1,0:T(4,128)S(1)} %pad_maximum_fusion.1), channel_id=1, source_target_pairs={{0,32},{8,40},{16,48},{24,56},{32,0},{40,8},{48,16},{56,24},{64,96... | collective-permute-start | bytes 394760 | tf_op jit(solution)/shard_map/ppermute | solution.py:20
  39.8 14.9 %collective-permute-start.2 = (f32[2,4,4,514]{3,2,1,0:T(4,128)S(1)}, f32[2,4,4,514]{3,2,1,0:T(4,128)S(1)}, u32[]{:S(2)}, u32[]{:S(2)}) collective-permute-start(f32[2,4,4,514]{3,2,1,0:T(4,128)S(1)} %pad_maximum_fusion.2), channel_id=1, source_target_pairs={{0,64},{8,72},{16,80},{24,88},{32,96},{40,104},{48,112},{56,120},{... | collective-permute-start | bytes 197384 | tf_op jit(solution)/shard_map/ppermute | solution.py:20
  55.5 15.7 %collective-permute-start.3 = (f32[4,4,514]{2,1,0:T(4,128)S(1)}, f32[4,4,514]{2,1,0:T(4,128)S(1)}, u32[]{:S(2)}, u32[]{:S(2)}) collective-permute-start(f32[4,4,514]{2,1,0:T(4,128)S(1)} %pad_maximum_fusion.3), channel_id=1, source_target_pairs={{0,128},{8,136},{16,144},{24,152},{32,160},{40,168},{48,176},{56,1... | collective-permute-start | bytes 98696 | tf_op jit(solution)/shard_map/ppermute | solution.py:20
  71.5 5.9 %collective-permute-start.4 = (f32[4,4,514]{2,1,0:T(4,128)S(1)}, f32[4,4,514]{2,1,0:T(4,128)S(1)}, u32[]{:S(2)}, u32[]{:S(2)}) collective-permute-start(f32[4,4,514]{2,1,0:T(4,128)S(1)} %pad_maximum_fusion.4), channel_id=1, source_target_pairs={{0,16},{8,24},{16,0},{24,8},{32,48},{40,56},{48,32},{56,40},{64,80... | collective-permute-start | bytes 98696 | tf_op jit(solution)/shard_map/ppermute | solution.py:20
  77.7 3.1 collective-permute-start.5
  81.5 3.2 collective-permute-start.6
  84.8 7.5 %collective-permute-start.7 = (f32[16,2048]{1,0:T(8,128)S(1)}, f32[16,2048]{1,0:T(8,128)S(1)}, u32[]{:S(2)}, u32[]{:S(2)}) collective-permute-start(f32[16,2048]{1,0:T(8,128)S(1)} %add.216), channel_id=1, source_target_pairs={{0,16},{8,24},{16,0},{24,8},{32,48},{40,56},{48,32},{56,40},{64,80... | collective-permute-start | bytes 393224 | tf_op jit(solution)/shard_map/ppermute | solution.py:20
  92.3 10.4 %collective-permute-start.8 = (f32[16,2048]{1,0:T(8,128)S(1)}, f32[16,2048]{1,0:T(8,128)S(1)}, u32[]{:S(2)}, u32[]{:S(2)}) collective-permute-start(f32[16,2048]{1,0:T(8,128)S(1)} %add.217), channel_id=1, source_target_pairs={{0,32},{8,40},{16,48},{24,56},{32,0},{40,8},{48,16},{56,24},{64,96... | collective-permute-start | bytes 393224 | tf_op jit(solution)/shard_map/ppermute | solution.py:20
  102.7 18.6 %collective-permute-start.9 = (f32[16,2048]{1,0:T(8,128)S(1)}, f32[16,2048]{1,0:T(8,128)S(1)}, u32[]{:S(2)}, u32[]{:S(2)}) collective-permute-start(f32[16,2048]{1,0:T(8,128)S(1)} %add.218), channel_id=1, source_target_pairs={{0,64},{8,72},{16,80},{24,88},{32,96},{40,104},{48,112},{56,120},{... | collective-permute-start | bytes 393224 | tf_op jit(solution)/shard_map/ppermute | solution.py:20
  121.3 22.9 %collective-permute-start.10 = (f32[16,2048]{1,0:T(8,128)S(1)}, f32[16,2048]{1,0:T(8,128)S(1)}, u32[]{:S(2)}, u32[]{:S(2)}) collective-permute-start(f32[16,2048]{1,0:T(8,128)S(1)} %add.219), channel_id=1, source_target_pairs={{0,128},{8,136},{16,144},{24,152},{32,160},{40,168},{48,176},{56,1... | collective-permute-start | bytes 393224 | tf_op jit(solution)/shard_map/ppermute | solution.py:20
  144.2 6.9 %collective-permute-start.11 = (f32[16,2048]{1,0:T(8,128)S(1)}, f32[16,2048]{1,0:T(8,128)S(1)}, u32[]{:S(2)}, u32[]{:S(2)}) collective-permute-start(f32[16,2048]{1,0:T(8,128)S(1)} %add.220), channel_id=1, source_target_pairs={{0,256},{8,264},{16,272},{24,280},{32,288},{40,296},{48,304},{56,3... | collective-permute-start | bytes 393224 | tf_op jit(solution)/shard_map/ppermute | solution.py:20
  325.7 3.2 collective-permute-start.12
  329.0 7.4 %collective-permute-start.13 = (f32[16,2048]{1,0:T(8,128)S(1)}, f32[16,2048]{1,0:T(8,128)S(1)}, u32[]{:S(2)}, u32[]{:S(2)}) collective-permute-start(f32[16,2048]{1,0:T(8,128)S(1)} %add.226), channel_id=1, source_target_pairs={{0,16},{8,24},{16,0},{24,8},{32,48},{40,56},{48,32},{56,40},{64,80... | collective-permute-start | bytes 393224 | tf_op jit(solution)/shard_map/ppermute | solution.py:20
  336.5 10.3 %collective-permute-start.14 = (f32[16,2048]{1,0:T(8,128)S(1)}, f32[16,2048]{1,0:T(8,128)S(1)}, u32[]{:S(2)}, u32[]{:S(2)}) collective-permute-start(f32[16,2048]{1,0:T(8,128)S(1)} %add.227), channel_id=1, source_target_pairs={{0,32},{8,40},{16,48},{24,56},{32,0},{40,8},{48,16},{56,24},{64,96... | collective-permute-start | bytes 393224 | tf_op jit(solution)/shard_map/ppermute | solution.py:20
  346.8 17.6 %collective-permute-start.15 = (f32[16,2048]{1,0:T(8,128)S(1)}, f32[16,2048]{1,0:T(8,128)S(1)}, u32[]{:S(2)}, u32[]{:S(2)}) collective-permute-start(f32[16,2048]{1,0:T(8,128)S(1)} %add.228), channel_id=1, source_target_pairs={{0,64},{8,72},{16,80},{24,88},{32,96},{40,104},{48,112},{56,120},{... | collective-permute-start | bytes 393224 | tf_op jit(solution)/shard_map/ppermute | solution.py:20
  364.4 24.0 %collective-permute-start.16 = (f32[16,2048]{1,0:T(8,128)S(1)}, f32[16,2048]{1,0:T(8,128)S(1)}, u32[]{:S(2)}, u32[]{:S(2)}) collective-permute-start(f32[16,2048]{1,0:T(8,128)S(1)} %add.229), channel_id=1, source_target_pairs={{0,128},{8,136},{16,144},{24,152},{32,160},{40,168},{48,176},{56,1... | collective-permute-start | bytes 393224 | tf_op jit(solution)/shard_map/ppermute | solution.py:20
  388.4 6.9 %collective-permute-start.17 = (f32[16,2048]{1,0:T(8,128)S(1)}, f32[16,2048]{1,0:T(8,128)S(1)}, u32[]{:S(2)}, u32[]{:S(2)}) collective-permute-start(f32[16,2048]{1,0:T(8,128)S(1)} %add.230), channel_id=1, source_target_pairs={{0,256},{8,264},{16,272},{24,280},{32,288},{40,296},{48,304},{56,3... | collective-permute-start | bytes 393224 | tf_op jit(solution)/shard_map/ppermute | solution.py:20
Sparse Core Ops, SparseCore 0:
  10.5 103.3 all-gather.3
  117.1 100.2 all-gather.5
  220.6 97.7 all-gather.7
where the time goes:
time: 403 us; the launch traced here: 402 us
  waiting for transfers between devices  266 us (66%)
  starting transfers between devices  96.2 us (24%)
  matrix products  15.7 us (4%)
  between operations  13.7 us (3%)
  local copies, waits for them, and re-layouts  6.86 us (2%)
    ppermute x18, waiting for transfers between devices, exchange(): lax.ppermute(part, axis, xor_pairs(count, mask))  102 us
    all_gather x1, waiting for transfers between devices, local(): down_w = lax.all_gather(w_down, 'exp', axis=1, tiled=True)  101 us
    ppermute x18, starting transfers between devices, exchange(): lax.ppermute(part, axis, xor_pairs(count, mask))  96.1 us
    all_gather x1, waiting for transfers between devices, local(): up_w = lax.all_gather(w_up, 'exp', axis=2, tiled=True)  61.2 us
  transfers between devices with their start and end apart: 21, of which 20 were waited for; matrix products, arithmetic and copies ran while one was open for 4% of the time, Pallas kernels for 0%

commit v1 on v0

--- a/solution.py
+++ b/solution.py
@@ -187,7 +187,9 @@
     ).astype(jnp.bfloat16)
     gate_w = lax.all_gather(w_gate, "exp", axis=2, tiled=True)
     up_w = lax.all_gather(w_up, "exp", axis=2, tiled=True)
-    down_w = lax.all_gather(w_down, "exp", axis=1, tiled=True)
+    down_w = jnp.concatenate(
+        lax.all_to_all(jnp.stack([w_down] * lax.axis_size("exp")), "exp", 0, 0), axis=1
+    )
     gate = jnp.einsum("erd,edf->erf", dispatched, gate_w, preferred_element_type=jnp.float32)
     upper = jnp.einsum("erd,edf->erf", dispatched, up_w, preferred_element_type=jnp.float32)
     hidden_all = (jax.nn.silu(gate) * upper).astype(jnp.bfloat16)

time: 403 us -> 362 us (0.90)
  waiting for transfers between devices: 266 us -> 217 us
  starting transfers between devices: 96.2 us -> 101 us
    all_gather x1 -> x0, waiting for transfers between devices: 101 us -> none  [local(): down_w = lax.all_gather(w_down, 'exp', axis=1, tiled=True)]
    all_gather x1, waiting for transfers between devices: 61.2 us -> 96.7 us  [local(): up_w = lax.all_gather(w_up, 'exp', axis=2, tiled=True)]
    all_gather x1, waiting for transfers between devices: 0.02 us -> 19.7 us  [local(): gate_w = lax.all_gather(w_gate, 'exp', axis=2, tiled=True)]
    all_to_all x0 -> x1, starting transfers between devices: none -> 4.85 us  [local(): lax.all_to_all(jnp.stack([w_down] * lax.axis_size('exp')), 'exp', 0, 0)]
  transfers between devices with their start and end apart: 21 -> 21, of which waited for: 20 -> 19; matrix products, arithmetic and copies ran while one was open for 4% -> 6% of each run, Pallas kernels for 0% -> 0%
where the time goes in v1:
time: 362 us; the launch traced here: 361 us
  waiting for transfers between devices  217 us (60%)
  starting transfers between devices  101 us (28%)
  matrix products  15.7 us (4%)
  between operations  14 us (4%)
  local copies, waits for them, and re-layouts  10.1 us (3%)
    ppermute x18, waiting for transfers between devices, exchange(): lax.ppermute(part, axis, xor_pairs(count, mask))  99.5 us
    all_gather x1, waiting for transfers between devices, local(): up_w = lax.all_gather(w_up, 'exp', axis=2, tiled=True)  96.7 us
    ppermute x18, starting transfers between devices, exchange(): lax.ppermute(part, axis, xor_pairs(count, mask))  95.7 us
    all_gather x1, waiting for transfers between devices, local(): gate_w = lax.all_gather(w_gate, 'exp', axis=2, tiled=True)  19.7 us
  transfers between devices with their start and end apart: 21, of which 19 were waited for; matrix products, arithmetic and copies ran while one was open for 6% of the time, Pallas kernels for 0%

profile of v1, /device:TPU:8, one launch (start us, length us, event | category | flops | bytes accessed | tf_op | source)
XLA Modules:
  0.0 361.3 jit_solution(1965306934168135428)
XLA Ops:
  6.5 0.7 all-gather.3.cloned.1.call-update
  7.3 0.7 all-gather.5.cloned.1.call-update
  8.0 0.7 broadcast_compare_fusion
  8.8 1.4 fusion.114
  10.1 1.2 fusion.112
  11.3 0.2 fusion.22
  11.5 0.3 fusion.24
  12.2 0.3 copy.117
  12.5 0.3 copy.142
  13.0 0.3 copy.116
  13.4 7.7 %collective-permute-start = (f32[2,2,2,4,4,514]{5,4,3,2,1,0:T(4,128)S(1)}, f32[2,2,2,4,4,514]{5,4,3,2,1,0:T(4,128)S(1)}, u32[]{:S(2)}, u32[]{:S(2)}) collective-permute-start(f32[2,2,2,4,4,514]{5,4,3,2,1,0:T(4,128)S(1)} %pad_maximum_fusion), channel_id=1, source_target_pairs={{0,256},{8,264},{16,272},{24,280},{32,288},{40,296},{48,304},{56,3... | collective-permute-start | bytes 789512 | tf_op jit(solution)/shard_map/ppermute | solution.py:20
  21.1 3.2 stack.2
  24.4 4.8 %all-to-all-start = ((bf16[8,1,176,2048]{3,2,1,0:T(8,128)(2,1)}), bf16[8,1,176,2048]{3,2,1,0:T(8,128)(2,1)}, u32[]{:S(2)}, u32[]{:S(2)}) async-start(bf16[8,1,176,2048]{3,2,1,0:T(8,128)(2,1)} %stack.2), calls=%async_computation | async-start | bytes 11534336 | tf_op jit(solution)/shard_map/all_to_all | solution.py:191
  29.3 1.0 constant_dynamic-slice_fusion.1
  30.3 0.2 fusion.109
  30.5 0.3 copy.145
  30.9 0.2 copy.121
  31.1 0.2 copy.122
  31.6 1.9 collective-permute-start.1
  33.6 6.5 %collective-permute-done.1 = f32[2,2,4,4,514]{4,3,2,1,0:T(4,128)S(1)} collective-permute-done((f32[2,2,4,4,514]{4,3,2,1,0:T(4,128)S(1)}, f32[2,2,4,4,514]{4,3,2,1,0:T(4,128)S(1)}, u32[]{:S(2)}, u32[]{:S(2)}) %collective-permute-start.1) | collective-permute-done | bytes 131616 | tf_op jit(solution)/shard_map/ppermute | solution.py:20
  41.1 9.1 %collective-permute-start.2 = (f32[2,4,4,514]{3,2,1,0:T(4,128)S(1)}, f32[2,4,4,514]{3,2,1,0:T(4,128)S(1)}, u32[]{:S(2)}, u32[]{:S(2)}) collective-permute-start(f32[2,4,4,514]{3,2,1,0:T(4,128)S(1)} %pad_maximum_fusion.2), channel_id=1, source_target_pairs={{0,64},{8,72},{16,80},{24,88},{32,96},{40,104},{48,112},{56,120},{... | collective-permute-start | bytes 197384 | tf_op jit(solution)/shard_map/ppermute | solution.py:20
  50.2 0.8 constant_dynamic-slice_fusion
  51.0 5.0 %collective-permute-done.2 = f32[2,4,4,514]{3,2,1,0:T(4,128)S(1)} collective-permute-done((f32[2,4,4,514]{3,2,1,0:T(4,128)S(1)}, f32[2,4,4,514]{3,2,1,0:T(4,128)S(1)}, u32[]{:S(2)}, u32[]{:S(2)}) %collective-permute-start.2) | collective-permute-done | bytes 65824 | tf_op jit(solution)/shard_map/ppermute | solution.py:20
  56.7 13.7 %collective-permute-start.3 = (f32[4,4,514]{2,1,0:T(4,128)S(1)}, f32[4,4,514]{2,1,0:T(4,128)S(1)}, u32[]{:S(2)}, u32[]{:S(2)}) collective-permute-start(f32[4,4,514]{2,1,0:T(4,128)S(1)} %pad_maximum_fusion.3), channel_id=1, source_target_pairs={{0,128},{8,136},{16,144},{24,152},{32,160},{40,168},{48,176},{56,1... | collective-permute-start | bytes 98696 | tf_op jit(solution)/shard_map/ppermute | solution.py:20
  70.7 1.7 collective-permute-done.3
  72.8 1.9 collective-permute-start.4
  74.8 3.8 %collective-permute-done.4 = f32[4,4,514]{2,1,0:T(4,128)S(1)} collective-permute-done((f32[4,4,514]{2,1,0:T(4,128)S(1)}, f32[4,4,514]{2,1,0:T(4,128)S(1)}, u32[]{:S(2)}, u32[]{:S(2)}) %collective-permute-start.4) | collective-permute-done | bytes 32928 | tf_op jit(solution)/shard_map/ppermute | solution.py:20
  79.0 1.9 collective-permute-start.5
  81.2 0.9 collective-permute-done.5
  82.3 0.2 fusion.37
  82.5 0.3 fusion.20
  82.8 2.1 collective-permute-start.6
  84.9 1.2 collective-permute-done.6
  86.0 1.9 collective-permute-start.7
  88.0 5.5 %collective-permute-done.7 = f32[16,2048]{1,0:T(8,128)S(1)} collective-permute-done((f32[16,2048]{1,0:T(8,128)S(1)}, f32[16,2048]{1,0:T(8,128)S(1)}, u32[]{:S(2)}, u32[]{:S(2)}) %collective-permute-start.7) | collective-permute-done | bytes 131104 | tf_op jit(solution)/shard_map/ppermute | solution.py:20
  93.5 1.9 collective-permute-start.8
  95.5 8.5 %collective-permute-done.8 = f32[16,2048]{1,0:T(8,128)S(1)} collective-permute-done((f32[16,2048]{1,0:T(8,128)S(1)}, f32[16,2048]{1,0:T(8,128)S(1)}, u32[]{:S(2)}, u32[]{:S(2)}) %collective-permute-start.8) | collective-permute-done | bytes 131104 | tf_op jit(solution)/shard_map/ppermute | solution.py:20
  104.0 6.4 %collective-permute-start.9 = (f32[16,2048]{1,0:T(8,128)S(1)}, f32[16,2048]{1,0:T(8,128)S(1)}, u32[]{:S(2)}, u32[]{:S(2)}) collective-permute-start(f32[16,2048]{1,0:T(8,128)S(1)} %add.218), channel_id=1, source_target_pairs={{0,64},{8,72},{16,80},{24,88},{32,96},{40,104},{48,112},{56,120},{... | collective-permute-start | bytes 393224 | tf_op jit(solution)/shard_map/ppermute | solution.py:20
  110.4 12.2 %collective-permute-done.9 = f32[16,2048]{1,0:T(8,128)S(1)} collective-permute-done((f32[16,2048]{1,0:T(8,128)S(1)}, f32[16,2048]{1,0:T(8,128)S(1)}, u32[]{:S(2)}, u32[]{:S(2)}) %collective-permute-start.9) | collective-permute-done | bytes 131104 | tf_op jit(solution)/shard_map/ppermute | solution.py:20
  122.6 10.5 %collective-permute-start.10 = (f32[16,2048]{1,0:T(8,128)S(1)}, f32[16,2048]{1,0:T(8,128)S(1)}, u32[]{:S(2)}, u32[]{:S(2)}) collective-permute-start(f32[16,2048]{1,0:T(8,128)S(1)} %add.219), channel_id=1, source_target_pairs={{0,128},{8,136},{16,144},{24,152},{32,160},{40,168},{48,176},{56,1... | collective-permute-start | bytes 393224 | tf_op jit(solution)/shard_map/ppermute | solution.py:20
  133.1 12.3 %collective-permute-done.10 = f32[16,2048]{1,0:T(8,128)S(1)} collective-permute-done((f32[16,2048]{1,0:T(8,128)S(1)}, f32[16,2048]{1,0:T(8,128)S(1)}, u32[]{:S(2)}, u32[]{:S(2)}) %collective-permute-start.10) | collective-permute-done | bytes 131104 | tf_op jit(solution)/shard_map/ppermute | solution.py:20
  145.5 3.8 %collective-permute-start.11 = (f32[16,2048]{1,0:T(8,128)S(1)}, f32[16,2048]{1,0:T(8,128)S(1)}, u32[]{:S(2)}, u32[]{:S(2)}) collective-permute-start(f32[16,2048]{1,0:T(8,128)S(1)} %add.220), channel_id=1, source_target_pairs={{0,256},{8,264},{16,272},{24,280},{32,288},{40,296},{48,304},{56,3... | collective-permute-start | bytes 393224 | tf_op jit(solution)/shard_map/ppermute | solution.py:20
  149.6 0.3 reduce_window_sum.11
  150.1 5.2 %collective-permute-done.11 = f32[16,2048]{1,0:T(8,128)S(1)} collective-permute-done((f32[16,2048]{1,0:T(8,128)S(1)}, f32[16,2048]{1,0:T(8,128)S(1)}, u32[]{:S(2)}, u32[]{:S(2)}) %collective-permute-start.11) | collective-permute-done | bytes 131104 | tf_op jit(solution)/shard_map/ppermute | solution.py:20
  155.5 0.2 fusion.17
  155.7 0.2 select_reduce_fusion
  156.2 19.7 %all-gather.3.cloned.1.call-done = bf16[1,2048,1408]{1,2,0:T(8,128)(2,1)} async-done(((bf16[1,2048,176]{1,2,0:T(8,128)(2,1)}), bf16[1,2048,1408]{1,2,0:T(8,128)(2,1)}) %all-gather.3.cloned.1.call-update) | async-done | bytes 5767184 | tf_op jit(solution)/shard_map/all_gather | solution.py:188
  175.9 4.2 %fusion.2 = f32[3,1408]{1,0:T(4,128)S(1)} fusion(bf16[3,2048]{1,0:T(4,128)(2,1)S(1)} %convolution_convert_fusion, bf16[1,2048,1408]{1,2,0:T(8,128)(2,1)} %all-gather.3.cloned.1.call-done), kind=kOutput, calls=%fused_computation.2 | convolution fusion | flops 17301504 | bytes 5796352 | tf_op jit(solution)/shard_map/erd,edf->erf/dot_general | solution.py:193
  180.1 96.7 %all-gather.5.cloned.1.call-done = bf16[1,2048,1408]{1,2,0:T(8,128)(2,1)} async-done(((bf16[1,2048,176]{1,2,0:T(8,128)(2,1)}), bf16[1,2048,1408]{1,2,0:T(8,128)(2,1)}) %all-gather.5.cloned.1.call-update) | async-done | bytes 5767184 | tf_op jit(solution)/shard_map/all_gather | solution.py:189
  276.9 7.0 %fusion.13 = f32[3,2048]{1,0:T(4,128)S(1)} fusion(bf16[1408,2048]{1,0:T(8,128)(2,1)} %bitcast.51, bf16[3,2048]{1,0:T(4,128)(2,1)S(1)} %convolution_convert_fusion, bf16[1,2048,1408]{1,2,0:T(8,128)(2,1)} %all-gather.5.cloned.1.call-done, f32[3,1408]{1,0:T(4,128)S(1)} %fusion.2), kind=kOutput, calls=%fused_computation.11 | convolution fusion | flops 34628352 | bytes 11588096 | tf_op jit(solution)/shard_map/erf,efd->erd/dot_general | solution.py:196
  283.9 0.4 fusion.115
  284.3 1.9 collective-permute-start.12
  286.2 1.3 collective-permute-done.12
  287.5 3.5 collective-permute-start.13
  291.0 4.0 %collective-permute-done.13 = f32[16,2048]{1,0:T(8,128)S(1)} collective-permute-done((f32[16,2048]{1,0:T(8,128)S(1)}, f32[16,2048]{1,0:T(8,128)S(1)}, u32[]{:S(2)}, u32[]{:S(2)}) %collective-permute-start.13) | collective-permute-done | bytes 131104 | tf_op jit(solution)/shard_map/ppermute | solution.py:20
  295.0 4.5 %collective-permute-start.14 = (f32[16,2048]{1,0:T(8,128)S(1)}, f32[16,2048]{1,0:T(8,128)S(1)}, u32[]{:S(2)}, u32[]{:S(2)}) collective-permute-start(f32[16,2048]{1,0:T(8,128)S(1)} %add.227), channel_id=1, source_target_pairs={{0,32},{8,40},{16,48},{24,56},{32,0},{40,8},{48,16},{56,24},{64,96... | collective-permute-start | bytes 393224 | tf_op jit(solution)/shard_map/ppermute | solution.py:20
  299.4 5.8 %collective-permute-done.14 = f32[16,2048]{1,0:T(8,128)S(1)} collective-permute-done((f32[16,2048]{1,0:T(8,128)S(1)}, f32[16,2048]{1,0:T(8,128)S(1)}, u32[]{:S(2)}, u32[]{:S(2)}) %collective-permute-start.14) | collective-permute-done | bytes 131104 | tf_op jit(solution)/shard_map/ppermute | solution.py:20
  305.3 7.6 %collective-permute-start.15 = (f32[16,2048]{1,0:T(8,128)S(1)}, f32[16,2048]{1,0:T(8,128)S(1)}, u32[]{:S(2)}, u32[]{:S(2)}) collective-permute-start(f32[16,2048]{1,0:T(8,128)S(1)} %add.228), channel_id=1, source_target_pairs={{0,64},{8,72},{16,80},{24,88},{32,96},{40,104},{48,112},{56,120},{... | collective-permute-start | bytes 393224 | tf_op jit(solution)/shard_map/ppermute | solution.py:20
  312.9 9.9 %collective-permute-done.15 = f32[16,2048]{1,0:T(8,128)S(1)} collective-permute-done((f32[16,2048]{1,0:T(8,128)S(1)}, f32[16,2048]{1,0:T(8,128)S(1)}, u32[]{:S(2)}, u32[]{:S(2)}) %collective-permute-start.15) | collective-permute-done | bytes 131104 | tf_op jit(solution)/shard_map/ppermute | solution.py:20
  322.9 12.0 %collective-permute-start.16 = (f32[16,2048]{1,0:T(8,128)S(1)}, f32[16,2048]{1,0:T(8,128)S(1)}, u32[]{:S(2)}, u32[]{:S(2)}) collective-permute-start(f32[16,2048]{1,0:T(8,128)S(1)} %add.229), channel_id=1, source_target_pairs={{0,128},{8,136},{16,144},{24,152},{32,160},{40,168},{48,176},{56,1... | collective-permute-start | bytes 393224 | tf_op jit(solution)/shard_map/ppermute | solution.py:20
  334.9 12.0 %collective-permute-done.16 = f32[16,2048]{1,0:T(8,128)S(1)} collective-permute-done((f32[16,2048]{1,0:T(8,128)S(1)}, f32[16,2048]{1,0:T(8,128)S(1)}, u32[]{:S(2)}, u32[]{:S(2)}) %collective-permute-start.16) | collective-permute-done | bytes 131104 | tf_op jit(solution)/shard_map/ppermute | solution.py:20
  346.9 3.3 collective-permute-start.17
  350.2 3.5 collective-permute-done.17
  353.8 0.7 reshape.309
  (104 shorter events, 5.2 us)
Async XLA Ops:
  6.5 2.2 copy-start
  6.5 14.6 %copy-start.1 = (bf16[1,176,2048]{2,1,0:T(8,128)(2,1)S(1)}, bf16[1,176,2048]{2,1,0:T(8,128)(2,1)}, u32[]{:S(2)}) copy-start(bf16[1,176,2048]{2,1,0:T(8,128)(2,1)} %param.31) | copy-start | bytes 2162692
  6.5 169.4 %all-gather.3.cloned.1.call-start = ((), (), s32[]{:S(2)}) async-start(), calls=%async_computation.1 | async-start | bytes 6488064 | tf_op jit(solution)/shard_map/all_gather | solution.py:188
  7.3 269.6 %all-gather.5.cloned.1.call-start = ((), (), s32[]{:S(2)}) async-start(), calls=%async_computation.2 | async-start | bytes 6488064 | tf_op jit(solution)/shard_map/all_gather | solution.py:189
  13.4 16.9 %collective-permute-start = (f32[2,2,2,4,4,514]{5,4,3,2,1,0:T(4,128)S(1)}, f32[2,2,2,4,4,514]{5,4,3,2,1,0:T(4,128)S(1)}, u32[]{:S(2)}, u32[]{:S(2)}) collective-permute-start(f32[2,2,2,4,4,514]{5,4,3,2,1,0:T(4,128)S(1)} %pad_maximum_fusion), channel_id=1, source_target_pairs={{0,256},{8,264},{16,272},{24,280},{32,288},{40,296},{48,304},{56,3... | collective-permute-start | bytes 789512 | tf_op jit(solution)/shard_map/ppermute | solution.py:20
  24.4 9.1 %copy-start.8 = (bf16[4,4,512]{2,1,0:T(4,128)(2,1)S(1)}, bf16[4,4,512]{2,1,0:T(4,128)(2,1)}, u32[]{:S(2)}) copy-start(bf16[4,4,512]{2,1,0:T(4,128)(2,1)} %param.19) | copy-start | bytes 49156
  24.4 50.3 %copy-start.9 = (bf16[4,4,64]{2,1,0:T(4,128)(2,1)S(1)}, bf16[4,4,64]{2,1,0:T(4,128)(2,1)}, u32[]{:S(2)}) copy-start(bf16[4,4,64]{2,1,0:T(4,128)(2,1)} %param.20) | copy-start | bytes 6148
  24.4 58.1 %copy-start.3 = (bf16[32,2048]{1,0:T(8,128)(2,1)S(1)}, bf16[32,2048]{1,0:T(8,128)(2,1)}, u32[]{:S(2)}) copy-start(bf16[32,2048]{1,0:T(8,128)(2,1)} %param.25) | copy-start | bytes 393220
  24.4 58.1 %copy-start.6 = (bf16[512,32]{0,1:T(8,128)(2,1)S(1)}, bf16[512,32]{0,1:T(8,128)(2,1)}, u32[]{:S(2)}) copy-start(bf16[512,32]{0,1:T(8,128)(2,1)} %param.24) | copy-start | bytes 98308
  24.4 155.8 %all-to-all-start = ((bf16[8,1,176,2048]{3,2,1,0:T(8,128)(2,1)}), bf16[8,1,176,2048]{3,2,1,0:T(8,128)(2,1)}, u32[]{:S(2)}, u32[]{:S(2)}) async-start(bf16[8,1,176,2048]{3,2,1,0:T(8,128)(2,1)} %stack.2), calls=%async_computation | async-start | bytes 11534336 | tf_op jit(solution)/shard_map/all_to_all | solution.py:191
  29.2 103.9 %copy-start.4 = (s32[4,4,6]{2,1,0:T(4,128)S(1)}, s32[4,4,6]{2,1,0:T(4,128)}, u32[]{:S(2)}) copy-start(s32[4,4,6]{2,1,0:T(4,128)} %param.28) | copy-start | bytes 1156
  29.3 120.2 %copy-start.5 = (bf16[4,4,2048]{2,1,0:T(4,128)(2,1)S(1)}, bf16[4,4,2048]{2,1,0:T(4,128)(2,1)}, u32[]{:S(2)}) copy-start(bf16[4,4,2048]{2,1,0:T(4,128)(2,1)} %param.16) | copy-start | bytes 196612
  29.3 126.2 %copy-start.2 = (bf16[2048,64]{0,1:T(8,128)(2,1)S(1)}, bf16[2048,64]{0,1:T(8,128)(2,1)}, u32[]{:S(2)}) copy-start(bf16[2048,64]{0,1:T(8,128)(2,1)} %param.27) | copy-start | bytes 786436
  29.3 126.2 %copy-start.7 = (f32[2048]{0:T(1024)S(1)}, f32[2048]{0:T(1024)}, u32[]{:S(2)}) copy-start(f32[2048]{0:T(1024)} %param.26) | copy-start | bytes 24580
  31.6 8.6 %collective-permute-start.1 = (f32[2,2,4,4,514]{4,3,2,1,0:T(4,128)S(1)}, f32[2,2,4,4,514]{4,3,2,1,0:T(4,128)S(1)}, u32[]{:S(2)}, u32[]{:S(2)}) collective-permute-start(f32[2,2,4,4,514]{4,3,2,1,0:T(4,128)S(1)} %pad_maximum_fusion.1), channel_id=1, source_target_pairs={{0,32},{8,40},{16,48},{24,56},{32,0},{40,8},{48,16},{56,24},{64,96... | collective-permute-start | bytes 394760 | tf_op jit(solution)/shard_map/ppermute | solution.py:20
  41.1 14.9 %collective-permute-start.2 = (f32[2,4,4,514]{3,2,1,0:T(4,128)S(1)}, f32[2,4,4,514]{3,2,1,0:T(4,128)S(1)}, u32[]{:S(2)}, u32[]{:S(2)}) collective-permute-start(f32[2,4,4,514]{3,2,1,0:T(4,128)S(1)} %pad_maximum_fusion.2), channel_id=1, source_target_pairs={{0,64},{8,72},{16,80},{24,88},{32,96},{40,104},{48,112},{56,120},{... | collective-permute-start | bytes 197384 | tf_op jit(solution)/shard_map/ppermute | solution.py:20
  56.7 15.7 %collective-permute-start.3 = (f32[4,4,514]{2,1,0:T(4,128)S(1)}, f32[4,4,514]{2,1,0:T(4,128)S(1)}, u32[]{:S(2)}, u32[]{:S(2)}) collective-permute-start(f32[4,4,514]{2,1,0:T(4,128)S(1)} %pad_maximum_fusion.3), channel_id=1, source_target_pairs={{0,128},{8,136},{16,144},{24,152},{32,160},{40,168},{48,176},{56,1... | collective-permute-start | bytes 98696 | tf_op jit(solution)/shard_map/ppermute | solution.py:20
  72.8 5.9 %collective-permute-start.4 = (f32[4,4,514]{2,1,0:T(4,128)S(1)}, f32[4,4,514]{2,1,0:T(4,128)S(1)}, u32[]{:S(2)}, u32[]{:S(2)}) collective-permute-start(f32[4,4,514]{2,1,0:T(4,128)S(1)} %pad_maximum_fusion.4), channel_id=1, source_target_pairs={{0,16},{8,24},{16,0},{24,8},{32,48},{40,56},{48,32},{56,40},{64,80... | collective-permute-start | bytes 98696 | tf_op jit(solution)/shard_map/ppermute | solution.py:20
  79.0 3.1 collective-permute-start.5
  82.8 3.2 collective-permute-start.6
  86.0 7.5 %collective-permute-start.7 = (f32[16,2048]{1,0:T(8,128)S(1)}, f32[16,2048]{1,0:T(8,128)S(1)}, u32[]{:S(2)}, u32[]{:S(2)}) collective-permute-start(f32[16,2048]{1,0:T(8,128)S(1)} %add.216), channel_id=1, source_target_pairs={{0,16},{8,24},{16,0},{24,8},{32,48},{40,56},{48,32},{56,40},{64,80... | collective-permute-start | bytes 393224 | tf_op jit(solution)/shard_map/ppermute | solution.py:20
  93.5 10.4 %collective-permute-start.8 = (f32[16,2048]{1,0:T(8,128)S(1)}, f32[16,2048]{1,0:T(8,128)S(1)}, u32[]{:S(2)}, u32[]{:S(2)}) collective-permute-start(f32[16,2048]{1,0:T(8,128)S(1)} %add.217), channel_id=1, source_target_pairs={{0,32},{8,40},{16,48},{24,56},{32,0},{40,8},{48,16},{56,24},{64,96... | collective-permute-start | bytes 393224 | tf_op jit(solution)/shard_map/ppermute | solution.py:20
  104.0 18.6 %collective-permute-start.9 = (f32[16,2048]{1,0:T(8,128)S(1)}, f32[16,2048]{1,0:T(8,128)S(1)}, u32[]{:S(2)}, u32[]{:S(2)}) collective-permute-start(f32[16,2048]{1,0:T(8,128)S(1)} %add.218), channel_id=1, source_target_pairs={{0,64},{8,72},{16,80},{24,88},{32,96},{40,104},{48,112},{56,120},{... | collective-permute-start | bytes 393224 | tf_op jit(solution)/shard_map/ppermute | solution.py:20
  122.6 22.9 %collective-permute-start.10 = (f32[16,2048]{1,0:T(8,128)S(1)}, f32[16,2048]{1,0:T(8,128)S(1)}, u32[]{:S(2)}, u32[]{:S(2)}) collective-permute-start(f32[16,2048]{1,0:T(8,128)S(1)} %add.219), channel_id=1, source_target_pairs={{0,128},{8,136},{16,144},{24,152},{32,160},{40,168},{48,176},{56,1... | collective-permute-start | bytes 393224 | tf_op jit(solution)/shard_map/ppermute | solution.py:20
  145.5 9.8 %collective-permute-start.11 = (f32[16,2048]{1,0:T(8,128)S(1)}, f32[16,2048]{1,0:T(8,128)S(1)}, u32[]{:S(2)}, u32[]{:S(2)}) collective-permute-start(f32[16,2048]{1,0:T(8,128)S(1)} %add.220), channel_id=1, source_target_pairs={{0,256},{8,264},{16,272},{24,280},{32,288},{40,296},{48,304},{56,3... | collective-permute-start | bytes 393224 | tf_op jit(solution)/shard_map/ppermute | solution.py:20
  284.3 3.2 collective-permute-start.12
  287.5 7.4 %collective-permute-start.13 = (f32[16,2048]{1,0:T(8,128)S(1)}, f32[16,2048]{1,0:T(8,128)S(1)}, u32[]{:S(2)}, u32[]{:S(2)}) collective-permute-start(f32[16,2048]{1,0:T(8,128)S(1)} %add.226), channel_id=1, source_target_pairs={{0,16},{8,24},{16,0},{24,8},{32,48},{40,56},{48,32},{56,40},{64,80... | collective-permute-start | bytes 393224 | tf_op jit(solution)/shard_map/ppermute | solution.py:20
  295.0 10.3 %collective-permute-start.14 = (f32[16,2048]{1,0:T(8,128)S(1)}, f32[16,2048]{1,0:T(8,128)S(1)}, u32[]{:S(2)}, u32[]{:S(2)}) collective-permute-start(f32[16,2048]{1,0:T(8,128)S(1)} %add.227), channel_id=1, source_target_pairs={{0,32},{8,40},{16,48},{24,56},{32,0},{40,8},{48,16},{56,24},{64,96... | collective-permute-start | bytes 393224 | tf_op jit(solution)/shard_map/ppermute | solution.py:20
  305.3 17.6 %collective-permute-start.15 = (f32[16,2048]{1,0:T(8,128)S(1)}, f32[16,2048]{1,0:T(8,128)S(1)}, u32[]{:S(2)}, u32[]{:S(2)}) collective-permute-start(f32[16,2048]{1,0:T(8,128)S(1)} %add.228), channel_id=1, source_target_pairs={{0,64},{8,72},{16,80},{24,88},{32,96},{40,104},{48,112},{56,120},{... | collective-permute-start | bytes 393224 | tf_op jit(solution)/shard_map/ppermute | solution.py:20
  322.9 24.0 %collective-permute-start.16 = (f32[16,2048]{1,0:T(8,128)S(1)}, f32[16,2048]{1,0:T(8,128)S(1)}, u32[]{:S(2)}, u32[]{:S(2)}) collective-permute-start(f32[16,2048]{1,0:T(8,128)S(1)} %add.229), channel_id=1, source_target_pairs={{0,128},{8,136},{16,144},{24,152},{32,160},{40,168},{48,176},{56,1... | collective-permute-start | bytes 393224 | tf_op jit(solution)/shard_map/ppermute | solution.py:20
  346.9 6.9 %collective-permute-start.17 = (f32[16,2048]{1,0:T(8,128)S(1)}, f32[16,2048]{1,0:T(8,128)S(1)}, u32[]{:S(2)}, u32[]{:S(2)}) collective-permute-start(f32[16,2048]{1,0:T(8,128)S(1)} %add.230), channel_id=1, source_target_pairs={{0,256},{8,264},{16,272},{24,280},{32,288},{40,296},{48,304},{56,3... | collective-permute-start | bytes 393224 | tf_op jit(solution)/shard_map/ppermute | solution.py:20
Sparse Core Ops, SparseCore 0:
  10.5 165.3 all-gather.2
  179.1 97.7 all-gather.4
